TPU v7x, 512 devices: a whole 4x4x16 slice. The times are simulated.
512 devices in a mesh: req: 128 (over y, z, core), tp: 4 (over x).
Axes of the slice: x: 4, y: 4, z: 16, core: 2. Of those that a mesh axis runs over, the one named last changes fastest.
Arguments:
- tokens: bfloat16 [131072, 3584], P('req', 'tp'), may hold values from -6 to 6
- key_value_weight: bfloat16 [3584, 1024], P('tp'), may hold values from -0.09375 to 0.09375
- adapter_down_maps: bfloat16 [128, 16, 3584], P('req', None, 'tp'), may hold values from -0.09375 to 0.09375
- adapter_up_maps: bfloat16 [128, 16, 1024], P('req', None, 'tp'), may hold values from -1.5 to 1.5
- block_adapter_ids: int32 [1024], P('req'), may hold values from 0 to 127, never falling along the last dimension, each value on 1 to 32 neighbouring positions
- block_live_rows: int32 [1024], P('req'), may hold values from 32 to 128
- adapter_storage_slot: int32 [128], replicated, may hold values from 0 to 127, each once
Outputs:
- keys_values: bfloat16 [131072, 1024], P('req', 'tp')
Inputs may be any that keep to these rules, and one draw needn't show every extreme that they name: `block_adapter_ids`: block ids never fall from one block to the next, every adapter id names at least one block, and one adapter names 32 blocks. `adapter_storage_slot`: each storage slot belongs to exactly one adapter.
All inputs are finite; a program needn't handle non-finite values.
Results may differ from a plain program's by a relative error of at most 0.003.
Values may be sent and summed in bfloat16 or wider, within the bound.
No kernel may reach another device: no remote copies, remote signals or barrier semaphores. Data moves between devices by JAX's collectives and lax.ppermute only.
A program may use at most 64 MiB of HBM per device.

v0:
```python
import jax
import jax.numpy as jnp
from jax import lax
from jax.sharding import PartitionSpec as P

adapter_scale = 0.5


def shards(
    tokens,
    key_value_weight,
    adapter_down_maps,
    adapter_up_maps,
    block_adapter_ids,
    block_live_rows,
    adapter_storage_slot,
):
    rows_dev, width_dev = tokens.shape
    blocks_dev = block_adapter_ids.shape[0]
    block_rows = rows_dev // blocks_dev
    local_columns = adapter_up_maps.shape[2]
    adapter_count = adapter_storage_slot.shape[0]
    matches = (
        block_adapter_ids[:, None] == jnp.arange(adapter_count, dtype=jnp.int32)[None, :]
    ).astype(jnp.int32)
    slot_ids = jnp.sum(matches * adapter_storage_slot[None, :], axis=1)
    pieces = (
        lax.all_gather(adapter_down_maps, "req", axis=0, tiled=True),
        lax.all_gather(adapter_up_maps, "req", axis=0, tiled=True),
    )
    piece_count = pieces[0].shape[0]
    chosen = (slot_ids[:, None] == jnp.arange(piece_count, dtype=jnp.int32)[None, :]).astype(
        jnp.bfloat16
    )
    a_part = jnp.einsum("bj,jrd->brd", chosen, pieces[0], preferred_element_type=jnp.float32)
    b_part = jnp.einsum("bj,jrc->brc", chosen, pieces[1], preferred_element_type=jnp.float32)
    chosen_down_maps = a_part.astype(jnp.bfloat16)
    chosen_up_maps = b_part.astype(jnp.bfloat16)
    features_all = lax.all_gather(tokens, "tp", axis=1, tiled=True)
    tp_index = lax.axis_index("tp")
    own_part = lax.dynamic_slice_in_dim(
        lax.all_gather(key_value_weight, "tp", axis=0, tiled=True),
        tp_index * local_columns,
        local_columns,
        1,
    )
    base_result = jnp.dot(features_all, own_part, preferred_element_type=jnp.float32)
    complete_down_maps = lax.all_gather(chosen_down_maps, "tp", axis=2, tiled=True)
    blocked_input = features_all.reshape(blocks_dev, block_rows, features_all.shape[1])
    rank_reduced = jnp.einsum(
        "qzo,qjo->qzj", blocked_input, complete_down_maps, preferred_element_type=jnp.float32
    )
    low_values = rank_reduced.astype(jnp.bfloat16)
    adapter_result = jnp.einsum(
        "bkr,brc->bkc", low_values, chosen_up_maps, preferred_element_type=jnp.float32
    ).reshape(rows_dev, local_columns)
    live_rows = (
        jnp.arange(block_rows, dtype=jnp.int32)[None, :] < block_live_rows[:, None]
    ).reshape(rows_dev, 1)
    adapted_output = base_result + adapter_scale * adapter_result
    return jnp.where(live_rows, adapted_output, jnp.zeros_like(adapted_output)).astype(jnp.bfloat16)


def solution(mesh):
    in_specs = (
        P("req", "tp"),
        P("tp", None),
        P("req", None, "tp"),
        P("req", None, "tp"),
        P("req"),
        P("req"),
        P(),
    )
    out_specs = P("req", "tp")
    return jax.shard_map(shards, mesh=mesh, in_specs=in_specs, out_specs=out_specs, check_vma=False)
```

profile of v0, /device:TPU:1, one launch (start us, length us, event | category | flops | bytes accessed | tf_op | source)
XLA Modules:
  0.0 465.4 jit_solution(3460865263811185851)
XLA Ops:
  6.5 0.0 all-gather.11.cloned.1.call-start
  6.5 0.7 all-gather.11.cloned.1.call-update
  7.3 0.0 all-gather.9.cloned.1.call-start
  7.3 0.7 all-gather.9.cloned.1.call-update
  8.0 0.0 all-gather.7.cloned.1.call-start
  8.1 0.7 all-gather.7.cloned.1.call-update
  8.7 0.0 all-gather.5.cloned.1.call-start
  8.8 0.5 all-gather.5.cloned.1.call-update
  9.3 0.9 select_reduce_fusion
  10.2 0.7 fusion.23
  10.9 136.2 %all-gather.11.cloned.1.call-done = bf16[128,16,256]{2,1,0:T(8,128)(2,1)} async-done(((bf16[1,16,256]{2,1,0:T(8,128)(2,1)}), bf16[128,16,256]{2,1,0:T(8,128)(2,1)}) %all-gather.11.cloned.1.call-update) | async-done | bytes 1048592 | tf_op jit(solution)/shard_map/all_gather | solution.py:29
  147.1 1.6 convolution_convert_fusion
  148.7 139.3 %all-gather.9.cloned.1.call-done = bf16[128,16,896]{2,1,0:T(8,128)(2,1)} async-done(((bf16[1,16,896]{2,1,0:T(8,128)(2,1)}), bf16[128,16,896]{2,1,0:T(8,128)(2,1)}) %all-gather.9.cloned.1.call-update) | async-done | bytes 3670032 | tf_op jit(solution)/shard_map/all_gather | solution.py:28
  287.9 3.0 fusion.16
  291.0 12.6 %all_gather.18 = bf16[8,16,3584]{2,0,1:T(8,128)(2,1)S(1)} all-gather(bf16[8,16,896]{2,0,1:T(8,128)(2,1)S(1)} %fusion.16), channel_id=1, replica_groups=mesh['req'=128,'tp'=4] {'tp'}, dimensions={2}, use_global_device_ids=true | all-gather | bytes 1146880 | tf_op jit(solution)/shard_map/all_gather | solution.py:48
  303.5 63.6 %all-gather.7.cloned.1.call-done = bf16[1024,3584]{1,0:T(8,128)(2,1)} async-done(((bf16[1024,896]{1,0:T(8,128)(2,1)}), bf16[1024,3584]{1,0:T(8,128)(2,1)}) %all-gather.7.cloned.1.call-update) | async-done | bytes 7340048 | tf_op jit(solution)/shard_map/all_gather | solution.py:39
  367.2 5.3 %convolution_multiply_fusion = f32[8,128,256]{2,1,0:T(8,128)S(1)} fusion(bf16[8,128,3584]{2,1,0:T(8,128)(2,1)} %bitcast.18, bf16[8,16,3584]{2,0,1:T(8,128)(2,1)S(1)} %all_gather.18, bf16[8,16,256]{2,0,1:T(8,128)(2,1)S(1)} %convolution_convert_fusion), kind=kOutput, calls=%fused_computation.5 | convolution fusion | flops 126107648 | bytes 9371648 | tf_op jit(solution)/shard_map/bkr,brc->bkc/dot_general | solution.py:54
  372.5 0.3 copy.18
  372.8 79.2 %all-gather.5.cloned.1.call-done = bf16[3584,1024]{1,0:T(8,128)(2,1)} async-done(((bf16[896,1024]{1,0:T(8,128)(2,1)}), bf16[3584,1024]{1,0:T(8,128)(2,1)}) %all-gather.5.cloned.1.call-update) | async-done | bytes 7340048 | tf_op jit(solution)/shard_map/all_gather | solution.py:42
  452.0 5.8 %fusion.13 = bf16[1024,256]{0,1:T(8,128)(2,1)S(1)} fusion(f32[1024,256]{0,1:T(8,128)S(1)} %copy.18, bf16[1024,3584]{1,0:T(8,128)(2,1)} %all-gather.7.cloned.1.call-done, bf16[3584,1024]{1,0:T(8,128)(2,1)} %all-gather.5.cloned.1.call-done, s32[]{:T(128)S(6)} %select_n.7, pred[1024]{0:T(1024)(128)(4,1)S(1)} %fusion.23), kind=kOutput, calls=%fused_computation.8 | convolution fusion | flops 1879834624 | bytes 10748932 | tf_op jit(solution)/shard_map/dot_general | solution.py:47
  457.8 1.0 copy.17
Async XLA Ops:
  6.5 140.5 %all-gather.11.cloned.1.call-start = ((), (), s32[]{:S(2)}) async-start(), calls=%async_computation.3 | async-start | bytes 1056768 | tf_op jit(solution)/shard_map/all_gather | solution.py:29
  7.3 280.7 %all-gather.9.cloned.1.call-start = ((), (), s32[]{:S(2)}) async-start(), calls=%async_computation.2 | async-start | bytes 3698688 | tf_op jit(solution)/shard_map/all_gather | solution.py:28
  8.0 359.1 %all-gather.7.cloned.1.call-start = ((), (), s32[]{:S(2)}) async-start(), calls=%async_computation.1 | async-start | bytes 9175040 | tf_op jit(solution)/shard_map/all_gather | solution.py:39
  8.7 443.3 %all-gather.5.cloned.1.call-start = ((), (), s32[]{:S(2)}) async-start(), calls=%async_computation | async-start | bytes 9175040 | tf_op jit(solution)/shard_map/all_gather | solution.py:42
Sparse Core Ops, SparseCore 0:
  10.3 136.7 all-gather.10
  150.1 137.7 all-gather.8
  290.1 77.0 all-gather.6
  369.1 82.8 all-gather.4
where the time goes:
time: 466 us; the launch traced here: 465 us
  waiting for transfers between devices  421 us (90%)
  matrix products  15.7 us (3%)
  between operations  13.2 us (3%)
  blocking collectives  12.6 us (3%)
    all_gather x1, waiting for transfers between devices, shards(): lax.all_gather(adapter_down_maps, 'req', axis=0, tiled=True)  139 us
    all_gather x1, waiting for transfers between devices, shards(): lax.all_gather(adapter_up_maps, 'req', axis=0, tiled=True)  136 us
    all_gather x1, waiting for transfers between devices, shards(): lax.all_gather(key_value_weight, 'tp', axis=0, tiled=True)  79.2 us
    all_gather x1, waiting for transfers between devices, shards(): features_all = lax.all_gather(tokens, 'tp', axis=1, tiled=True)  63.6 us
    all_gather x1, blocking collectives, shards(): lax.all_gather(chosen_down_maps, 'tp', axis=2, tiled=True)  12.6 us
  transfers between devices with their start and end apart: 4, of which 4 were waited for; matrix products, arithmetic and copies ran while one was open for 3% of the time, Pallas kernels for 0%

commit v1 on v0

--- a/solution.py
+++ b/solution.py
@@ -26,7 +26,9 @@
     slot_ids = jnp.sum(matches * adapter_storage_slot[None, :], axis=1)
     pieces = (
         lax.all_gather(adapter_down_maps, "req", axis=0, tiled=True),
-        lax.all_gather(adapter_up_maps, "req", axis=0, tiled=True),
+        jnp.concatenate(
+            lax.all_to_all(jnp.stack([adapter_up_maps] * lax.axis_size("req")), "req", 0, 0), axis=0
+        ),
     )
     piece_count = pieces[0].shape[0]
     chosen = (slot_ids[:, None] == jnp.arange(piece_count, dtype=jnp.int32)[None, :]).astype(

time: 466 us -> 339 us (0.73)
  waiting for transfers between devices: 421 us -> 273 us
  starting transfers between devices: 0.12 us -> 20.6 us
    all_gather x1 -> x0, waiting for transfers between devices: 136 us -> none  [shards(): lax.all_gather(adapter_up_maps, 'req', axis=0, tiled=True)]
    all_gather x1, waiting for transfers between devices: 139 us -> 73.3 us  [shards(): lax.all_gather(adapter_down_maps, 'req', axis=0, tiled=True)]
    all_to_all x0 -> x1, waiting for transfers between devices: none -> 55 us  [shards(): lax.all_to_all(jnp.stack([adapter_up_maps] * lax.axis_size('req')), 'req'...]
    all_to_all x0 -> x1, starting transfers between devices: none -> 20.6 us  [shards(): lax.all_to_all(jnp.stack([adapter_up_maps] * lax.axis_size('req')), 'req'...]
  transfers between devices with their start and end apart: 4 -> 4, of which waited for: 4 -> 4; matrix products, arithmetic and copies ran while one was open for 3% -> 4% of each run, Pallas kernels for 0% -> 0%
where the time goes in v1:
time: 339 us
  waiting for transfers between devices  273 us (81%)
  starting transfers between devices  20.6 us (6%)
  matrix products  14.5 us (4%)
  between operations  13.1 us (4%)
  blocking collectives  12.6 us (4%)
    all_gather x1, waiting for transfers between devices, shards(): lax.all_gather(key_value_weight, 'tp', axis=0, tiled=True)  79.4 us
    all_gather x1, waiting for transfers between devices, shards(): lax.all_gather(adapter_down_maps, 'req', axis=0, tiled=True)  73.3 us
    all_gather x1, waiting for transfers between devices, shards(): features_all = lax.all_gather(tokens, 'tp', axis=1, tiled=True)  63.6 us
    all_to_all x1, waiting for transfers between devices, shards(): lax.all_to_all(jnp.stack([adapter_up_maps] * lax.axis_size('req')), 'req'...  55 us
    all_to_all x1, starting transfers between devices, shards(): lax.all_to_all(jnp.stack([adapter_up_maps] * lax.axis_size('req')), 'req'...  20.6 us
    all_gather x1, blocking collectives, shards(): lax.all_gather(chosen_down_maps, 'tp', axis=2, tiled=True)  12.6 us
  transfers between devices with their start and end apart: 4, of which 4 were waited for; matrix products, arithmetic and copies ran while one was open for 4% of the time, Pallas kernels for 0%

profile of v1, /device:TPU:1, one launch (start us, length us, event | category | flops | bytes accessed | tf_op | source)
XLA Modules:
  0.0 338.8 jit_solution(14111409945763071766)
XLA Ops:
  6.5 0.0 all-gather.8.cloned.1.call-start
  6.5 0.7 all-gather.8.cloned.1.call-update
  7.3 0.0 all-gather.6.cloned.1.call-start
  7.3 0.7 all-gather.6.cloned.1.call-update
  8.0 0.0 all-gather.4.cloned.1.call-start
  8.1 0.7 all-gather.4.cloned.1.call-update
  8.7 1.7 stack.2
  10.5 20.6 %all-to-all-start = ((bf16[128,1,16,256]{3,2,1,0:T(8,128)(2,1)}), bf16[128,1,16,256]{3,2,1,0:T(8,128)(2,1)S(1)}, u32[]{:S(2)}, u32[]{:S(2)}) async-start(bf16[128,1,16,256]{3,2,1,0:T(8,128)(2,1)} %stack.2), calls=%async_computation | async-start | bytes 2097152 | tf_op jit(solution)/shard_map/all_to_all | solution.py:30
  31.0 0.9 select_reduce_fusion
  31.9 0.7 fusion.24
  32.6 55.0 %all-to-all-done = bf16[128,1,16,256]{3,2,1,0:T(8,128)(2,1)S(1)} async-done(((bf16[128,1,16,256]{3,2,1,0:T(8,128)(2,1)}), bf16[128,1,16,256]{3,2,1,0:T(8,128)(2,1)S(1)}, u32[]{:S(2)}, u32[]{:S(2)}) %all-to-all-start) | async-done | bytes 1048608 | tf_op jit(solution)/shard_map/all_to_all | solution.py:30
  87.6 0.4 convolution_convert_fusion
  88.0 73.3 %all-gather.8.cloned.1.call-done = bf16[128,16,896]{2,1,0:T(8,128)(2,1)} async-done(((bf16[1,16,896]{2,1,0:T(8,128)(2,1)}), bf16[128,16,896]{2,1,0:T(8,128)(2,1)}) %all-gather.8.cloned.1.call-update) | async-done | bytes 3670032 | tf_op jit(solution)/shard_map/all_gather | solution.py:28
  161.3 3.0 fusion.16
  164.3 12.6 %all_gather.15 = bf16[8,16,3584]{2,0,1:T(8,128)(2,1)S(1)} all-gather(bf16[8,16,896]{2,0,1:T(8,128)(2,1)S(1)} %fusion.16), channel_id=1, replica_groups=mesh['req'=128,'tp'=4] {'tp'}, dimensions={2}, use_global_device_ids=true | all-gather | bytes 1146880 | tf_op jit(solution)/shard_map/all_gather | solution.py:50
  176.9 63.6 %all-gather.6.cloned.1.call-done = bf16[1024,3584]{1,0:T(8,128)(2,1)} async-done(((bf16[1024,896]{1,0:T(8,128)(2,1)}), bf16[1024,3584]{1,0:T(8,128)(2,1)}) %all-gather.6.cloned.1.call-update) | async-done | bytes 7340048 | tf_op jit(solution)/shard_map/all_gather | solution.py:41
  240.5 5.3 %convolution_multiply_fusion = f32[8,128,256]{2,1,0:T(8,128)S(1)} fusion(bf16[8,128,3584]{2,1,0:T(8,128)(2,1)} %bitcast.22, bf16[8,16,3584]{2,0,1:T(8,128)(2,1)S(1)} %all_gather.15, bf16[8,16,256]{2,0,1:T(8,128)(2,1)S(1)} %convolution_convert_fusion), kind=kOutput, calls=%fused_computation.5 | convolution fusion | flops 126107648 | bytes 9371648 | tf_op jit(solution)/shard_map/bkr,brc->bkc/dot_general | solution.py:56
  245.8 0.3 copy.23
  246.2 79.4 %all-gather.4.cloned.1.call-done = bf16[3584,1024]{1,0:T(8,128)(2,1)} async-done(((bf16[896,1024]{1,0:T(8,128)(2,1)}), bf16[3584,1024]{1,0:T(8,128)(2,1)}) %all-gather.4.cloned.1.call-update) | async-done | bytes 7340048 | tf_op jit(solution)/shard_map/all_gather | solution.py:44
  325.5 5.8 %fusion.13 = bf16[1024,256]{0,1:T(8,128)(2,1)S(1)} fusion(f32[1024,256]{0,1:T(8,128)S(1)} %copy.23, bf16[1024,3584]{1,0:T(8,128)(2,1)} %all-gather.6.cloned.1.call-done, bf16[3584,1024]{1,0:T(8,128)(2,1)} %all-gather.4.cloned.1.call-done, s32[]{:T(128)S(6)} %select_n.7, pred[1024]{0:T(1024)(128)(4,1)S(1)} %fusion.24), kind=kOutput, calls=%fused_computation.8 | convolution fusion | flops 1879834624 | bytes 10748932 | tf_op jit(solution)/shard_map/dot_general | solution.py:49
  331.3 1.0 copy.22
Async XLA Ops:
  6.5 154.7 %all-gather.8.cloned.1.call-start = ((), (), s32[]{:S(2)}) async-start(), calls=%async_computation.3 | async-start | bytes 3698688 | tf_op jit(solution)/shard_map/all_gather | solution.py:28
  7.3 233.2 %all-gather.6.cloned.1.call-start = ((), (), s32[]{:S(2)}) async-start(), calls=%async_computation.2 | async-start | bytes 9175040 | tf_op jit(solution)/shard_map/all_gather | solution.py:41
  8.0 317.5 %all-gather.4.cloned.1.call-start = ((), (), s32[]{:S(2)}) async-start(), calls=%async_computation.1 | async-start | bytes 9175040 | tf_op jit(solution)/shard_map/all_gather | solution.py:44
  10.5 77.1 %all-to-all-start = ((bf16[128,1,16,256]{3,2,1,0:T(8,128)(2,1)}), bf16[128,1,16,256]{3,2,1,0:T(8,128)(2,1)S(1)}, u32[]{:S(2)}, u32[]{:S(2)}) async-start(bf16[128,1,16,256]{3,2,1,0:T(8,128)(2,1)} %stack.2), calls=%async_computation | async-start | bytes 2097152 | tf_op jit(solution)/shard_map/all_to_all | solution.py:30
Sparse Core Ops, SparseCore 0:
  10.4 150.8 all-gather.7
  163.4 77.0 all-gather.5
  242.6 82.8 all-gather.3

commit v2 on v0

--- a/solution.py
+++ b/solution.py
@@ -4,6 +4,22 @@
 from jax.sharding import PartitionSpec as P
 
 adapter_scale = 0.5
+
+
+def gather_around(x, axis, dim):
+    ways, here, step = (lax.axis_size(axis), lax.axis_index(axis), x.shape[dim])
+    dims = [n * ways if d == dim else n for d, n in enumerate(x.shape)]
+    full = lax.dynamic_update_slice_in_dim(jnp.zeros(dims, x.dtype), x, here * step, axis=dim)
+    going_up = going_down = x
+    for far in range(1, ways // 2 + 1):
+        going_up = lax.ppermute(going_up, axis, [(d, (d + 1) % ways) for d in range(ways)])
+        full = lax.dynamic_update_slice_in_dim(full, going_up, (here - far) % ways * step, axis=dim)
+        if 2 * far < ways:
+            going_down = lax.ppermute(going_down, axis, [(d, (d - 1) % ways) for d in range(ways)])
+            full = lax.dynamic_update_slice_in_dim(
+                full, going_down, (here + far) % ways * step, axis=dim
+            )
+    return full
 
 
 def shards(
@@ -39,10 +55,7 @@
     features_all = lax.all_gather(tokens, "tp", axis=1, tiled=True)
     tp_index = lax.axis_index("tp")
     own_part = lax.dynamic_slice_in_dim(
-        lax.all_gather(key_value_weight, "tp", axis=0, tiled=True),
-        tp_index * local_columns,
-        local_columns,
-        1,
+        gather_around(key_value_weight, "tp", 0), tp_index * local_columns, local_columns, 1
     )
     base_result = jnp.dot(features_all, own_part, preferred_element_type=jnp.float32)
     complete_down_maps = lax.all_gather(chosen_down_maps, "tp", axis=2, tiled=True)

time: 466 us -> 387 us (0.83)
  waiting for transfers between devices: 421 us -> 315 us
  local copies, waits for them, and re-layouts: 1.33 us -> 15.4 us
  starting transfers between devices: 0.12 us -> 13.8 us
    all_gather x1 -> x0, waiting for transfers between devices: 79.2 us -> none  [shards(): lax.all_gather(key_value_weight, 'tp', axis=0, tiled=True)]
    all_gather x1, waiting for transfers between devices: 136 us -> 80.2 us  [shards(): lax.all_gather(adapter_up_maps, 'req', axis=0, tiled=True)]
    ppermute x0 -> x3, waiting for transfers between devices: none -> 32.3 us  [the longest x2 32.3 us: gather_around(): lax.ppermute(going_up, axis, [(d, (d + 1) % ways) for d in range(ways)])]
    ppermute x0 -> x3, starting transfers between devices: none -> 13.8 us  [the longest x2 10.6 us: gather_around(): lax.ppermute(going_up, axis, [(d, (d + 1) % ways) for d in range(ways)])]
    dynamic_update_slice x0 -> x4, local copies, waits for them, and re-layouts: none -> 10.1 us  [the longest x2 5.78 us: gather_around(): lax.dynamic_update_slice_in_dim(full, going_up, (here - far) % ways * ste...]
  transfers between devices with their start and end apart: 4 -> 6, of which waited for: 4 -> 4; matrix products, arithmetic and copies ran while one was open for 3% -> 5% of each run, Pallas kernels for 0% -> 0%
where the time goes in v2:
time: 387 us; the launch traced here: 386 us
  waiting for transfers between devices  315 us (81%)
  matrix products  15.8 us (4%)
  local copies, waits for them, and re-layouts  15.4 us (4%)
  starting transfers between devices  13.8 us (4%)
  between operations  13.2 us (3%)
  blocking collectives  12.6 us (3%)
    all_gather x1, waiting for transfers between devices, shards(): lax.all_gather(adapter_down_maps, 'req', axis=0, tiled=True)  136 us
    all_gather x1, waiting for transfers between devices, shards(): lax.all_gather(adapter_up_maps, 'req', axis=0, tiled=True)  80.2 us
    all_gather x1, waiting for transfers between devices, shards(): features_all = lax.all_gather(tokens, 'tp', axis=1, tiled=True)  63.6 us
    ppermute x2, waiting for transfers between devices, gather_around(): lax.ppermute(going_up, axis, [(d, (d + 1) % ways) for d in range(ways)])  32.3 us
    all_gather x1, blocking collectives, shards(): lax.all_gather(chosen_down_maps, 'tp', axis=2, tiled=True)  12.6 us
    ppermute x2, starting transfers between devices, gather_around(): lax.ppermute(going_up, axis, [(d, (d + 1) % ways) for d in range(ways)])  10.6 us
  transfers between devices with their start and end apart: 6, of which 4 were waited for; matrix products, arithmetic and copies ran while one was open for 5% of the time, Pallas kernels for 0%

profile of v2, /device:TPU:1, one launch (start us, length us, event | category | flops | bytes accessed | tf_op | source)
XLA Modules:
  0.0 386.2 jit_solution(13510352539915977908)
XLA Ops:
  6.5 0.0 copy-start
  6.5 0.0 all-gather.8.cloned.1.call-start
  6.5 0.7 all-gather.8.cloned.1.call-update
  7.3 0.0 all-gather.6.cloned.1.call-start
  7.3 0.7 all-gather.6.cloned.1.call-update
  8.0 0.0 all-gather.4.cloned.1.call-start
  8.1 0.7 all-gather.4.cloned.1.call-update
  8.7 3.9 %collective-permute-start = (bf16[896,1024]{1,0:T(8,128)(2,1)}, bf16[896,1024]{1,0:T(8,128)(2,1)}, u32[]{:S(2)}, u32[]{:S(2)}) collective-permute-start(bf16[896,1024]{1,0:T(8,128)(2,1)} %param.8), channel_id=1, source_target_pairs={{0,1},{1,2},{2,3},{3,0},{4,5},{5,6},{6,7},{7,4},{8,9},{9,10},{10,1... | collective-permute-start | bytes 5505032 | tf_op jit(solution)/shard_map/ppermute | solution.py:15
  12.7 3.2 collective-permute-start.1
  15.9 32.3 %collective-permute-done = bf16[896,1024]{1,0:T(8,128)(2,1)} collective-permute-done((bf16[896,1024]{1,0:T(8,128)(2,1)}, bf16[896,1024]{1,0:T(8,128)(2,1)}, u32[]{:S(2)}, u32[]{:S(2)}) %collective-permute-start) | collective-permute-done | bytes 1835040 | tf_op jit(solution)/shard_map/ppermute | solution.py:15
  48.2 6.6 %collective-permute-start.2 = (bf16[896,1024]{1,0:T(8,128)(2,1)}, bf16[896,1024]{1,0:T(8,128)(2,1)}, u32[]{:S(2)}, u32[]{:S(2)}) collective-permute-start(bf16[896,1024]{1,0:T(8,128)(2,1)} %collective-permute-done), channel_id=1, source_target_pairs={{0,1},{1,2},{2,3},{3,0},{4,5},{5,6},{6,7},{7,4},{8,9},{9,10},{10,1... | collective-permute-start | bytes 5505032 | tf_op jit(solution)/shard_map/ppermute | solution.py:15
  54.9 0.9 select_reduce_fusion
  55.7 3.9 %broadcast_in_dim.10 = bf16[3584,1024]{1,0:T(8,128)(2,1)} broadcast(bf16[]{:T(256)} %constant.34.clone.1), dimensions={} | broadcast | bytes 7340034 | tf_op jit(solution)/shard_map/broadcast_in_dim | solution.py:12
  59.7 0.0 copy-done
  59.7 1.4 constant_dynamic-update-slice_fusion.3
  61.1 0.0 copy-done.1
  61.1 0.1 fusion.23
  61.2 2.9 constant_dynamic-update-slice_fusion.2
  64.1 0.0 collective-permute-done.1
  64.1 2.9 constant_dynamic-update-slice_fusion.1
  66.9 80.2 %all-gather.8.cloned.1.call-done = bf16[128,16,256]{2,1,0:T(8,128)(2,1)} async-done(((bf16[1,16,256]{2,1,0:T(8,128)(2,1)}), bf16[128,16,256]{2,1,0:T(8,128)(2,1)}) %all-gather.8.cloned.1.call-update) | async-done | bytes 1048592 | tf_op jit(solution)/shard_map/all_gather | solution.py:45
  147.1 1.6 convolution_convert_fusion
  148.7 0.0 collective-permute-done.2
  148.7 2.9 constant_dynamic-update-slice_fusion
  151.6 136.4 %all-gather.6.cloned.1.call-done = bf16[128,16,896]{2,1,0:T(8,128)(2,1)} async-done(((bf16[1,16,896]{2,1,0:T(8,128)(2,1)}), bf16[128,16,896]{2,1,0:T(8,128)(2,1)}) %all-gather.6.cloned.1.call-update) | async-done | bytes 3670032 | tf_op jit(solution)/shard_map/all_gather | solution.py:44
  288.0 3.0 fusion.16
  291.0 12.6 %all_gather.14 = bf16[8,16,3584]{2,0,1:T(8,128)(2,1)S(1)} all-gather(bf16[8,16,896]{2,0,1:T(8,128)(2,1)S(1)} %fusion.16), channel_id=1, replica_groups=mesh['req'=128,'tp'=4] {'tp'}, dimensions={2}, use_global_device_ids=true | all-gather | bytes 1146880 | tf_op jit(solution)/shard_map/all_gather | solution.py:61
  303.6 63.6 %all-gather.4.cloned.1.call-done = bf16[1024,3584]{1,0:T(8,128)(2,1)} async-done(((bf16[1024,896]{1,0:T(8,128)(2,1)}), bf16[1024,3584]{1,0:T(8,128)(2,1)}) %all-gather.4.cloned.1.call-update) | async-done | bytes 7340048 | tf_op jit(solution)/shard_map/all_gather | solution.py:55
  367.2 5.3 %convolution_multiply_fusion = f32[8,128,256]{2,1,0:T(8,128)S(1)} fusion(bf16[8,128,3584]{2,1,0:T(8,128)(2,1)} %bitcast.18, bf16[8,16,3584]{2,0,1:T(8,128)(2,1)S(1)} %all_gather.14, bf16[8,16,256]{2,0,1:T(8,128)(2,1)S(1)} %convolution_convert_fusion), kind=kOutput, calls=%fused_computation.5 | convolution fusion | flops 126107648 | bytes 9371648 | tf_op jit(solution)/shard_map/bkr,brc->bkc/dot_general | solution.py:67
  372.6 0.3 copy.18
  372.9 5.8 %fusion.13 = bf16[1024,256]{0,1:T(8,128)(2,1)S(1)} fusion(f32[1024,256]{0,1:T(8,128)S(1)} %copy.18, bf16[1024,3584]{1,0:T(8,128)(2,1)} %all-gather.4.cloned.1.call-done, bf16[3584,1024]{1,0:T(8,128)(2,1)} %constant_dynamic-update-slice_fusion, s32[]{:T(128)S(6)} %select_n.41, pred[1024]{0:T(1024)(128)(4,1)S(1)} %fusion.23), kind=kOutput, calls=%fused_computation.8 | convolution fusion | flops 1879834624 | bytes 10748932 | tf_op jit(solution)/shard_map/dot_general | solution.py:60
  378.7 1.0 copy.17
  (1 shorter events, 0.0 us)
Async XLA Ops:
  6.5 53.1 %copy-start = (bf16[896,1024]{1,0:T(8,128)(2,1)S(1)}, bf16[896,1024]{1,0:T(8,128)(2,1)}, u32[]{:S(2)}) copy-start(bf16[896,1024]{1,0:T(8,128)(2,1)} %param.8) | copy-start | bytes 5505028
  6.5 54.6 %copy-start.1 = (s32[8]{0:T(128)S(1)}, s32[8]{0:T(128)}, u32[]{:S(2)}) copy-start(s32[8]{0:T(128)} %param.12) | copy-start | bytes 100
  6.5 140.6 %all-gather.8.cloned.1.call-start = ((), (), s32[]{:S(2)}) async-start(), calls=%async_computation.2 | async-start | bytes 1056768 | tf_op jit(solution)/shard_map/all_gather | solution.py:45
  7.3 280.7 %all-gather.6.cloned.1.call-start = ((), (), s32[]{:S(2)}) async-start(), calls=%async_computation.1 | async-start | bytes 3698688 | tf_op jit(solution)/shard_map/all_gather | solution.py:44
  8.0 359.2 %all-gather.4.cloned.1.call-start = ((), (), s32[]{:S(2)}) async-start(), calls=%async_computation | async-start | bytes 9175040 | tf_op jit(solution)/shard_map/all_gather | solution.py:55
  8.7 39.4 %collective-permute-start = (bf16[896,1024]{1,0:T(8,128)(2,1)}, bf16[896,1024]{1,0:T(8,128)(2,1)}, u32[]{:S(2)}, u32[]{:S(2)}) collective-permute-start(bf16[896,1024]{1,0:T(8,128)(2,1)} %param.8), channel_id=1, source_target_pairs={{0,1},{1,2},{2,3},{3,0},{4,5},{5,6},{6,7},{7,4},{8,9},{9,10},{10,1... | collective-permute-start | bytes 5505032 | tf_op jit(solution)/shard_map/ppermute | solution.py:15
  12.7 51.4 %collective-permute-start.1 = (bf16[896,1024]{1,0:T(8,128)(2,1)}, bf16[896,1024]{1,0:T(8,128)(2,1)}, u32[]{:S(2)}, u32[]{:S(2)}) collective-permute-start(bf16[896,1024]{1,0:T(8,128)(2,1)} %param.8), channel_id=1, source_target_pairs={{0,3},{1,0},{2,1},{3,2},{4,7},{5,4},{6,5},{7,6},{8,11},{9,8},{10,9... | collective-permute-start | bytes 5505032 | tf_op jit(solution)/shard_map/ppermute | solution.py:18
  48.2 100.5 %collective-permute-start.2 = (bf16[896,1024]{1,0:T(8,128)(2,1)}, bf16[896,1024]{1,0:T(8,128)(2,1)}, u32[]{:S(2)}, u32[]{:S(2)}) collective-permute-start(bf16[896,1024]{1,0:T(8,128)(2,1)} %collective-permute-done), channel_id=1, source_target_pairs={{0,1},{1,2},{2,3},{3,0},{4,5},{5,6},{6,7},{7,4},{8,9},{9,10},{10,1... | collective-permute-start | bytes 5505032 | tf_op jit(solution)/shard_map/ppermute | solution.py:15
Sparse Core Ops, SparseCore 0:
  10.3 136.7 all-gather.7
  150.1 137.8 all-gather.5
  290.1 77.0 all-gather.3
